TPU v7x, 256 devices: a whole 4x4x8 slice. The times are simulated.
256 devices in a mesh: req: 64 (over y_lo, z, x), tp: 4 (over y_hi, core).
Axes of the slice: x: 4, y: 4 (y_hi: 2, y_lo: 2; y = y_hi * 2 + y_lo), z: 8, core: 2. Of those that a mesh axis runs over, the one named last changes fastest.
Arguments:
- query_heads: bfloat16 [61440, 4096], P('req', 'tp'), parts along dimension 0, may hold values from -140 to 140
- normed_key_heads: bfloat16 [61440, 512], P('req', 'tp'), parts along dimension 0, may hold values from -7 to 7
- value_rows_per_head: bfloat16 [61440, 512], P('req', 'tp'), parts along dimension 0, may hold values from -6 to 6
- residual_in: bfloat16 [61440, 2048], P(('req', 'tp')), parts along dimension 0, may hold values from -6 to 6
- out_weight: bfloat16 [4096, 2048], P('tp'), may hold values from -0.09375 to 0.09375
- norm_gain: float32 [2048], replicated, may hold values from 0.3 to 3
- gate_up: bfloat16 [2, 2, 2048, 768], P(None, None, None, 'tp'), may hold values from -0.125 to 0.125
- down_weight: bfloat16 [2, 768, 2048], P(None, 'tp'), may hold values from -0.21875 to 0.21875
- segment_ids: int32 [61440], P('req'), parts along dimension 0, may hold values from 0 to 5, never falling along the last dimension, each value on 1 to 480 neighbouring positions
- expert_ids: int32 [61440, 8], P('req'), parts along dimension 0, may hold values from 0 to 127, all different within a row; in each aligned block of 960 rows (0 to 959, 960 to 1919, ...) at most 75 rows name the same one
- gate_weights: float32 [61440, 8], P('req'), parts along dimension 0, may hold values from 0.05 to 0.8
Outputs:
- layer_out: bfloat16 [61440, 2048], P(('req', 'tp')), parts along dimension 0
There are 64 independent parts, one for each index of `req`. A program takes and returns all parts, laid end to end along the dimension named above; an argument that names none is the same for every part. Nothing has to cross between parts.
Inputs may be any that keep to these rules, and one draw needn't show every extreme that they name: `segment_ids`: segment ids never fall along the tokens; each prompt has 1 to 480 tokens and one has exactly 480. `expert_ids`: the 8 experts of a token are distinct; no expert is chosen by more than 75 tokens of a request group, a bound that some block reaches.
All inputs are finite; a program needn't handle non-finite values.
Results may differ from a plain program's by a relative error of at most 0.0053.
Values may be sent and summed in bfloat16 or wider, within the bound.
No kernel may reach another device: no remote copies, remote signals or barrier semaphores. Data moves between devices by JAX's collectives and lax.ppermute only.
A program may use at most 128 MiB of HBM per device.

v0:
```python
import math
import jax
import jax.numpy as jnp
from jax import lax
from jax.sharding import PartitionSpec as P

QUERY_HEADS = 32
KEY_VALUE_HEADS = 4
HEAD_WIDTH = 128
EXPERTS = 128


def positions_of(segment_ids):
    earlier = (segment_ids[None, :] < segment_ids[:, None]).astype(jnp.int32)
    return jnp.arange(segment_ids.shape[0], dtype=jnp.int32) - jnp.sum(earlier, axis=1)


def rotary_tables(vectors, token_positions):
    half_dim = vectors.shape[-1] // 2
    frequency = 1000000.0 ** (-jnp.arange(half_dim, dtype=jnp.float32) / half_dim)
    angles = token_positions.astype(jnp.float32)[:, None] * frequency[None, :]
    cosine = jnp.cos(angles)[:, None, :]
    sine = jnp.sin(angles)[:, None, :]
    first = vectors[..., :half_dim]
    second = vectors[..., half_dim:]
    return jnp.concatenate(
        [first * cosine - second * sine, second * cosine + first * sine], axis=-1
    )


def rms_norm(hidden, gain):
    widened = hidden.astype(jnp.float32)
    factor = lax.rsqrt(jnp.mean(widened * widened, axis=-1, keepdims=True) + 1e-06)
    return (widened * factor * gain).astype(jnp.bfloat16)


def compact(chosen, limit):
    total = chosen.shape[0]
    iota = jnp.arange(total, dtype=jnp.int32)
    ranked = jnp.where(chosen, iota, iota + total)
    order = jnp.argsort(ranked, stable=True)[:limit]
    return (order, chosen[order])


def attend(query_heads, normed_key_heads, value_rows_per_head, segment_ids):
    item_count = segment_ids.shape[0]
    token_positions = positions_of(segment_ids)
    kv_local = normed_key_heads.shape[1] // HEAD_WIDTH
    query_group_width = QUERY_HEADS // KEY_VALUE_HEADS
    queries = rotary_tables(
        query_heads.reshape(item_count, kv_local * query_group_width, HEAD_WIDTH).astype(
            jnp.float32
        ),
        token_positions,
    ).astype(jnp.bfloat16)
    keys_after_rotary = rotary_tables(
        normed_key_heads.reshape(item_count, kv_local, HEAD_WIDTH).astype(jnp.float32),
        token_positions,
    ).astype(jnp.bfloat16)
    values = value_rows_per_head.reshape(item_count, kv_local, HEAD_WIDTH)
    indices = jnp.arange(item_count)
    allowed = (segment_ids[:, None] == segment_ids[None, :]) & (
        indices[None, :] <= indices[:, None]
    )
    factor = 1.0 / math.sqrt(HEAD_WIDTH)
    key_one = keys_after_rotary[:, 0]
    value_one = values[:, 0]

    def one_head(query_one, key_one=key_one, value_one=value_one):
        scores = jnp.dot(query_one, key_one.T, preferred_element_type=jnp.float32) * factor
        scores = jnp.where(allowed, scores, -1e30)
        peak = jnp.max(scores, axis=1, keepdims=True)
        weights = jnp.exp(scores - peak)
        weights = (weights / jnp.sum(weights, axis=1, keepdims=True)).astype(jnp.bfloat16)
        return jnp.dot(weights, value_one, preferred_element_type=jnp.float32).astype(jnp.bfloat16)

    group_queries = queries.transpose(1, 0, 2)
    blocks = lax.map(one_head, group_queries)
    attended = blocks.transpose(1, 0, 2)
    return attended.reshape(item_count, kv_local * query_group_width * HEAD_WIDTH)


def local(
    query_heads,
    normed_key_heads,
    value_rows_per_head,
    residual_in,
    out_weight,
    norm_gain,
    gate_up,
    down_weight,
    segment_ids,
    expert_ids,
    gate_weights,
):
    attended = attend(query_heads, normed_key_heads, value_rows_per_head, segment_ids)
    tok_rows = residual_in.shape[0]
    width = residual_in.shape[1]
    group_tokens = expert_ids.shape[0]
    capacity = group_tokens * expert_ids.shape[1] * 5 // (EXPERTS * 4)
    window = gate_up.shape[0]
    slots = jnp.arange(window, dtype=jnp.int32)
    route_all = jnp.sum(
        jnp.where(expert_ids[:, :, None] == slots[None, None, :], gate_weights[:, :, None], 0.0),
        axis=1,
    )
    normed_all = None
    rows = attended
    projected = lax.psum_scatter(
        jnp.dot(rows, out_weight, preferred_element_type=jnp.float32),
        "tp",
        scatter_dimension=0,
        tiled=True,
    )
    mixed = (residual_in.astype(jnp.float32) + projected).astype(jnp.bfloat16)
    normed = rms_norm(mixed, norm_gain)
    normed_all = lax.all_gather(normed, "tp", axis=0, tiled=True)
    rows = normed_all
    limit = min(capacity, tok_rows * lax.axis_size("tp"))
    summed = jnp.zeros((tok_rows * lax.axis_size("tp"), width), jnp.float32)
    for expert in range(window):
        taken, valid = compact(jnp.any(expert_ids == expert, axis=1), limit)
        picked = rows[taken]
        gate = jnp.dot(picked, gate_up[expert, 0], preferred_element_type=jnp.float32)
        upward = jnp.dot(picked, gate_up[expert, 1], preferred_element_type=jnp.float32)
        active = (jax.nn.silu(gate) * upward).astype(jnp.bfloat16)
        outputs = jnp.dot(active, down_weight[expert], preferred_element_type=jnp.float32)
        scale = jnp.where(valid, route_all[taken, expert], 0.0)
        summed = summed.at[taken].add(scale[:, None] * outputs)
    experts = lax.psum_scatter(summed, "tp", scatter_dimension=0, tiled=True)
    return (mixed.astype(jnp.float32) + experts).astype(jnp.bfloat16)


def solution(mesh):
    placed = (
        P("req", "tp"),
        P("req", "tp"),
        P("req", "tp"),
        P(("req", "tp"), None),
        P("tp", None),
        P(),
        P(None, None, None, "tp"),
        P(None, "tp", None),
        P("req"),
        P("req", None),
        P("req", None),
    )
    return jax.shard_map(
        local, mesh=mesh, in_specs=placed, out_specs=P(("req", "tp"), None), check_vma=False
    )
```

profile of v0, /device:TPU:1, one launch (start us, length us, event | category | flops | bytes accessed | tf_op | source)
XLA Modules:
  0.0 299.4 jit_solution(11987907407622865133)
XLA Ops:
  6.6 1.4 convert_reduce_fusion
  8.0 1.0 bitcast_convert_fusion
  9.0 1.8 multiply_cosine_fusion.1
  10.7 2.3 fusion.49
  13.0 0.4 convert_bitcast_fusion
  13.5 0.9 copy.25
  14.4 1.5 subtract_convert_fusion
  15.9 1.1 maximum_bitcast_fusion
  17.0 0.0 copy-start.4
  17.0 0.3 copy.22
  17.3 0.1 pad_maximum_fusion
  17.5 0.3 copy-done.4
  17.7 0.3 copy-done.6
  18.0 25.1 %while.11 = (s32[]{:T(128)}, bf16[8,960,128]{2,1,0:T(8,128)(2,1)}, bf16[8,960,128]{2,1,0:T(8,128)(2,1)S(1)}, bf16[960,128]{1,0:T(8,128)(2,1)S(1)}, bf16[960,128]...) while((s32[]{:T(128)}, bf16[8,960,128]{2,1,0:T(8,128)(2,1)}, ...), condition=%wide.region_4.5_spmd.clone, body=%wide.region_1.4_spmd.clone.sunk | while | flops 482117760 | bytes 12069725 | solution.py:78
  18.0 1.0 fusion.81
  19.0 0.6 fusion.82
  19.6 1.5 fusion.83
  21.1 1.0 fusion.81
  22.1 0.6 fusion.82
  22.7 1.5 fusion.83
  24.3 1.0 fusion.81
  25.2 0.6 fusion.82
  25.8 1.6 fusion.83
  27.4 1.0 fusion.81
  28.4 0.6 fusion.82
  29.0 1.6 fusion.83
  30.6 1.0 fusion.81
  31.6 0.6 fusion.82
  32.1 1.6 fusion.83
  33.7 1.0 fusion.81
  34.7 0.6 fusion.82
  35.3 1.6 fusion.83
  36.9 1.0 fusion.81
  37.9 0.6 fusion.82
  38.4 1.6 fusion.83
  40.0 1.0 fusion.81
  41.0 0.6 fusion.82
  41.6 1.5 fusion.83
  43.1 10.1 %fusion.17 = f32[960,2048]{1,0:T(8,128)} fusion(bf16[1024,2048]{1,0:T(8,128)(2,1)} %param.17, bf16[8,960,128]{2,1,0:T(8,128)(2,1)} %get-tuple-element.39), kind=kOutput, calls=%fused_computation.37 | convolution fusion | flops 4026531840 | bytes 14024704 | tf_op jit(solution)/shard_map/dot_general | solution.py:110
  53.2 0.0 reduce-scatter.3.cloned.1.call-update
  53.3 0.2 all-gather.2.cloned.1.call-start
  53.5 85.1 %reduce-scatter.3.cloned.1.call-done = f32[240,2048]{1,0:T(8,128)} async-done(((f32[960,2048]{1,0:T(8,128)}), f32[240,2048]{1,0:T(8,128)}) %reduce-scatter.3.cloned.1.call-update) | async-done | bytes 1966096 | tf_op jit(solution)/shard_map/reduce_scatter | solution.py:109
  138.6 1.9 fusion.13
  140.5 1.2 fusion.15
  141.8 0.0 all-gather.2.cloned.1.call-update
  141.8 0.0 reduce-scatter.5.cloned.1.call-start
  141.9 4.4 %sort.32 = (s32[960]{0:T(1024)}, s32[960]{0:T(1024)S(1)}) sort(s32[960]{0:T(1024)S(1)} %get-tuple-element.103, s32[960]{0:T(1024)S(1)} %iota.47), dimensions={0}, to_apply=%region_12.13 | sort | flops 9600 | bytes 15360 | tf_op jit(solution)/shard_map/jit(argsort)/sort | solution.py:41
  146.3 1.3 gather_fusion.3
  147.6 2.0 gather_fusion.4
  149.7 4.4 %sort.31 = (s32[960]{0:T(1024)}, s32[960]{0:T(1024)S(1)}) sort(s32[960]{0:T(1024)S(1)} %get-tuple-element.104, s32[960]{0:T(1024)S(1)} %iota.45), dimensions={0}, to_apply=%region_7.8 | sort | flops 9600 | bytes 15360 | tf_op jit(solution)/shard_map/jit(argsort)/sort | solution.py:41
  154.0 2.0 gather_fusion.1
  156.1 1.3 gather_fusion
  157.4 24.6 %all-gather.2.cloned.1.call-done = bf16[960,2048]{1,0:T(8,128)(2,1)} async-done(((bf16[240,2048]{1,0:T(8,128)(2,1)}), bf16[960,2048]{1,0:T(8,128)(2,1)}) %all-gather.2.cloned.1.call-update) | async-done | bytes 3932176 | tf_op jit(solution)/shard_map/all_gather | solution.py:117
  182.0 3.7 %gather_fusion.2 = bf16[75,2048]{1,0:T(8,128)(2,1)S(1)} fusion(bf16[960,2048]{1,0:T(8,128)(2,1)} %all-gather.2.cloned.1.call-done, s32[1024]{0:T(1024)S(1)} %pad_clamp_fusion.1), kind=kCustom, calls=%fused_computation.2 | custom fusion | bytes 614700 | tf_op jit(solution)/shard_map/gather | solution.py:123
  185.7 1.5 fusion.30
  187.2 3.7 %gather_fusion.5 = bf16[75,2048]{1,0:T(8,128)(2,1)S(1)} fusion(bf16[960,2048]{1,0:T(8,128)(2,1)} %all-gather.2.cloned.1.call-done, s32[1024]{0:T(1024)S(1)} %pad_clamp_fusion), kind=kCustom, calls=%fused_computation.5 | custom fusion | bytes 614700 | tf_op jit(solution)/shard_map/gather | solution.py:123
  190.9 1.5 fusion.25
  192.4 2.1 convolution_multiply_fusion
  194.6 2.1 convolution_multiply_fusion.1
  196.7 5.0 %scatter_custom_fusion = f32[960,2048]{1,0:T(8,128)} fusion(s32[75]{0:T(128)S(1)} %get-tuple-element.92, f32[75,2048]{1,0:T(8,128)S(1)} %convolution_multiply_fusion.1, f32[]{:T(128)} %constant.16.clone.1), kind=kCustom, calls=%fused_computation.23 | custom fusion | flops 153600 | bytes 7864324 | tf_op jit(solution)/shard_map/scatter-add | solution.py:129
  201.8 7.8 %scatter_fusion = f32[960,2048]{1,0:T(8,128)} fusion(f32[960,2048]{1,0:T(8,128)} %scatter_custom_fusion, s32[75]{0:T(128)S(1)} %get-tuple-element.90, f32[75,2048]{1,0:T(8,128)S(1)} %convolution_multiply_fusion), kind=kCustom, calls=%fused_computation.7 | custom fusion | flops 153600 | bytes 1843500 | tf_op jit(solution)/shard_map/scatter-add | solution.py:129
  209.5 0.0 reduce-scatter.5.cloned.1.call-update
  209.6 80.6 %reduce-scatter.5.cloned.1.call-done = f32[240,2048]{1,0:T(8,128)} async-done(((f32[960,2048]{1,0:T(8,128)}), f32[240,2048]{1,0:T(8,128)}) %reduce-scatter.5.cloned.1.call-update) | async-done | bytes 1966096 | tf_op jit(solution)/shard_map/reduce_scatter | solution.py:130
  290.1 2.7 fusion.16
  (27 shorter events, 0.2 us)
Async XLA Ops:
  6.5 6.5 %copy-start = (bf16[960,1024]{1,0:T(8,128)(2,1)S(1)}, bf16[960,1024]{1,0:T(8,128)(2,1)}, u32[]{:S(2)}) copy-start(bf16[960,1024]{1,0:T(8,128)(2,1)} %param.13) | copy-start | bytes 5898244
  6.5 132.1 %reduce-scatter.3.cloned.1.call-start = ((), (), s32[]{:S(2)}) async-start(), calls=%async_computation.2 | async-start | bytes 9830400 | tf_op jit(solution)/shard_map/reduce_scatter | solution.py:109
  17.0 0.7 copy-start.4
  17.0 1.0 copy-start.6
  53.2 85.4 %copy-start.1 = (bf16[240,2048]{1,0:T(8,128)(2,1)S(1)}, bf16[240,2048]{1,0:T(8,128)(2,1)}, u32[]{:S(2)}) copy-start(bf16[240,2048]{1,0:T(8,128)(2,1)} %param.16) | copy-start | bytes 2949124
  53.2 87.3 %copy-start.5 = (f32[2048]{0:T(1024)S(1)}, f32[2048]{0:T(1024)}, u32[]{:S(2)}) copy-start(f32[2048]{0:T(1024)} %param.18) | copy-start | bytes 24580
  53.2 88.6 %copy-start.2 = (s32[960,8]{0,1:T(8,128)S(1)}, s32[960,8]{0,1:T(8,128)}, u32[]{:S(2)}) copy-start(s32[960,8]{0,1:T(8,128)} %param.22) | copy-start | bytes 92164
  53.3 94.3 %copy-start.3 = (f32[960,8]{0,1:T(8,128)S(1)}, f32[960,8]{0,1:T(8,128)}, u32[]{:S(2)}) copy-start(f32[960,8]{0,1:T(8,128)} %param.23) | copy-start | bytes 92164
  53.3 128.8 %all-gather.2.cloned.1.call-start = ((), (), s32[]{:S(2)}) async-start(), calls=%async_computation.3 | async-start | bytes 4915200 | tf_op jit(solution)/shard_map/all_gather | solution.py:117
  141.8 148.3 %reduce-scatter.5.cloned.1.call-start = ((), (), s32[]{:S(2)}) async-start(), calls=%async_computation.4 | async-start | bytes 9830400 | tf_op jit(solution)/shard_map/reduce_scatter | solution.py:130
Sparse Core Ops, SparseCore 0:
  53.4 85.1 reduce-scatter.2
  141.9 40.0 all-gather.1
  209.7 80.3 reduce-scatter.4
where the time goes:
time: 300 us; the launch traced here: 299 us
  waiting for transfers between devices  190 us (63%)
  other arithmetic  41.9 us (14%)
  matrix products  37.7 us (13%)
  local copies, waits for them, and re-layouts  15.8 us (5%)
  between operations  13.4 us (4%)
    reduce_scatter x1, waiting for transfers between devices, local(): lax.psum_scatter(jnp.dot(rows, out_weight, preferred_element_type=jnp.flo...  85.1 us
    reduce_scatter x1, waiting for transfers between devices, local(): experts = lax.psum_scatter(summed, 'tp', scatter_dimension=0, tiled=True)  80.6 us
    all_gather x1, waiting for transfers between devices, local(): normed_all = lax.all_gather(normed, 'tp', axis=0, tiled=True)  24.6 us
    scatter-add x2, other arithmetic, local(): summed = summed.at[taken].add(scale[:, None] * outputs)  12.8 us
    dot_general x8, matrix products, one_head(): jnp.dot(weights, value_one, preferred_element_type=jnp.float32)  12.4 us
    dot_general x1, matrix products, local(): jnp.dot(rows, out_weight, preferred_element_type=jnp.float32)  10.1 us
    sort x2, other arithmetic, compact(): order = jnp.argsort(ranked, stable=True)[:limit]  8.71 us
    dot_general x8, matrix products, one_head(): jnp.dot(query_one, key_one.T, preferred_element_type=jnp.float32) * factor  7.91 us
  transfers between devices with their start and end apart: 3, of which 3 were waited for; matrix products, arithmetic and copies ran while one was open for 5% of the time, Pallas kernels for 0%

commit v1 on v0

--- a/solution.py
+++ b/solution.py
@@ -114,7 +114,9 @@
     )
     mixed = (residual_in.astype(jnp.float32) + projected).astype(jnp.bfloat16)
     normed = rms_norm(mixed, norm_gain)
-    normed_all = lax.all_gather(normed, "tp", axis=0, tiled=True)
+    normed_all = jnp.concatenate(
+        lax.all_to_all(jnp.stack([normed] * lax.axis_size("tp")), "tp", 0, 0), axis=0
+    )
     rows = normed_all
     limit = min(capacity, tok_rows * lax.axis_size("tp"))
     summed = jnp.zeros((tok_rows * lax.axis_size("tp"), width), jnp.float32)

time: 300 us -> 313 us (1.043)
  waiting for transfers between devices: 190 us -> 196 us
  starting transfers between devices: 0.27 us -> 5.73 us
    all_to_all x0 -> x1, waiting for transfers between devices: none -> 30.2 us  [local(): lax.all_to_all(jnp.stack([normed] * lax.axis_size('tp')), 'tp', 0, 0)]
    all_gather x1 -> x0, waiting for transfers between devices: 24.6 us -> none  [local(): normed_all = lax.all_gather(normed, 'tp', axis=0, tiled=True)]
    all_to_all x0 -> x1, starting transfers between devices: none -> 5.73 us  [local(): lax.all_to_all(jnp.stack([normed] * lax.axis_size('tp')), 'tp', 0, 0)]
where the time goes in v1:
time: 313 us
  waiting for transfers between devices  196 us (63%)
  other arithmetic  41.1 us (13%)
  matrix products  37.8 us (12%)
  local copies, waits for them, and re-layouts  18.4 us (6%)
  between operations  13.7 us (4%)
  starting transfers between devices  5.73 us (2%)
    reduce_scatter x1, waiting for transfers between devices, local(): lax.psum_scatter(jnp.dot(rows, out_weight, preferred_element_type=jnp.flo...  85.3 us
    reduce_scatter x1, waiting for transfers between devices, local(): experts = lax.psum_scatter(summed, 'tp', scatter_dimension=0, tiled=True)  80.7 us
    all_to_all x1, waiting for transfers between devices, local(): lax.all_to_all(jnp.stack([normed] * lax.axis_size('tp')), 'tp', 0, 0)  30.2 us
    scatter-add x2, other arithmetic, local(): summed = summed.at[taken].add(scale[:, None] * outputs)  12.8 us
    dot_general x8, matrix products, one_head(): jnp.dot(weights, value_one, preferred_element_type=jnp.float32)  12.4 us
    dot_general x1, matrix products, local(): jnp.dot(rows, out_weight, preferred_element_type=jnp.float32)  10.1 us
    sort x2, other arithmetic, compact(): order = jnp.argsort(ranked, stable=True)[:limit]  8.74 us
    dot_general x8, matrix products, one_head(): jnp.dot(query_one, key_one.T, preferred_element_type=jnp.float32) * factor  7.93 us
  transfers between devices with their start and end apart: 3, of which 3 were waited for; matrix products, arithmetic and copies ran while one was open for 5% of the time, Pallas kernels for 0%

profile of v1, /device:TPU:1, one launch (start us, length us, event | category | flops | bytes accessed | tf_op | source)
XLA Modules:
  0.0 312.9 jit_solution(3286251207151563673)
XLA Ops:
  6.6 1.4 convert_reduce_fusion
  8.0 1.0 bitcast_convert_fusion
  9.0 1.8 multiply_cosine_fusion.1
  10.7 2.5 fusion.49
  13.2 0.4 convert_bitcast_fusion
  13.7 0.9 copy.25
  14.6 1.5 subtract_convert_fusion
  16.1 1.1 maximum_bitcast_fusion
  17.2 0.0 copy-start.4
  17.2 0.0 copy-start.6
  17.2 0.3 copy.22
  17.5 0.1 pad_maximum_fusion
  17.6 0.3 copy-done.4
  17.9 0.3 copy-done.6
  18.2 25.1 %while.11 = (s32[]{:T(128)}, bf16[8,960,128]{2,1,0:T(8,128)(2,1)}, bf16[8,960,128]{2,1,0:T(8,128)(2,1)S(1)}, bf16[960,128]{1,0:T(8,128)(2,1)S(1)}, bf16[960,128]...) while((s32[]{:T(128)}, bf16[8,960,128]{2,1,0:T(8,128)(2,1)}, ...), condition=%wide.region_4.5_spmd.clone, body=%wide.region_1.4_spmd.clone.sunk | while | flops 482117760 | bytes 12069725 | solution.py:78
  18.2 1.0 fusion.81
  19.2 0.6 fusion.82
  19.8 1.5 fusion.83
  21.3 1.0 fusion.81
  22.3 0.6 fusion.82
  22.9 1.6 fusion.83
  24.5 1.0 fusion.81
  25.4 0.6 fusion.82
  26.0 1.6 fusion.83
  27.6 1.0 fusion.81
  28.6 0.6 fusion.82
  29.2 1.6 fusion.83
  30.8 1.0 fusion.81
  31.7 0.6 fusion.82
  32.3 1.6 fusion.83
  33.9 1.0 fusion.81
  34.9 0.6 fusion.82
  35.5 1.6 fusion.83
  37.1 1.0 fusion.81
  38.0 0.6 fusion.82
  38.6 1.6 fusion.83
  40.2 1.0 fusion.81
  41.2 0.6 fusion.82
  41.8 1.5 fusion.83
  43.3 10.1 %fusion.17 = f32[960,2048]{1,0:T(8,128)} fusion(bf16[1024,2048]{1,0:T(8,128)(2,1)} %param.17, bf16[8,960,128]{2,1,0:T(8,128)(2,1)} %get-tuple-element.39), kind=kOutput, calls=%fused_computation.37 | convolution fusion | flops 4026531840 | bytes 14024704 | tf_op jit(solution)/shard_map/dot_general | solution.py:110
  53.4 0.0 reduce-scatter.3.cloned.1.call-update
  53.4 85.3 %reduce-scatter.3.cloned.1.call-done = f32[240,2048]{1,0:T(8,128)} async-done(((f32[960,2048]{1,0:T(8,128)}), f32[240,2048]{1,0:T(8,128)}) %reduce-scatter.3.cloned.1.call-update) | async-done | bytes 1966096 | tf_op jit(solution)/shard_map/reduce_scatter | solution.py:109
  138.8 1.9 fusion.13
  140.7 0.3 fusion.15
  141.0 2.4 stack.2
  143.4 5.7 %all-to-all-start = ((bf16[4,240,2048]{2,1,0:T(8,128)(2,1)}), bf16[4,240,2048]{2,1,0:T(8,128)(2,1)}, u32[]{:S(2)}, u32[]{:S(2)}) async-start(bf16[4,240,2048]{2,1,0:T(8,128)(2,1)} %stack.2), calls=%async_computation.1 | async-start | bytes 7864320 | tf_op jit(solution)/shard_map/all_to_all | solution.py:118
  149.2 4.4 %sort.32 = (s32[960]{0:T(1024)}, s32[960]{0:T(1024)S(1)}) sort(s32[960]{0:T(1024)S(1)} %get-tuple-element.103, s32[960]{0:T(1024)S(1)} %iota.47), dimensions={0}, to_apply=%region_12.13 | sort | flops 9600 | bytes 15360 | tf_op jit(solution)/shard_map/jit(argsort)/sort | solution.py:41
  153.6 1.5 gather_fusion.3
  155.1 2.0 gather_fusion.4
  157.2 4.4 %sort.31 = (s32[960]{0:T(1024)}, s32[960]{0:T(1024)S(1)}) sort(s32[960]{0:T(1024)S(1)} %get-tuple-element.104, s32[960]{0:T(1024)S(1)} %iota.45), dimensions={0}, to_apply=%region_7.8 | sort | flops 9600 | bytes 15360 | tf_op jit(solution)/shard_map/jit(argsort)/sort | solution.py:41
  161.5 2.0 gather_fusion.1
  163.6 1.3 gather_fusion
  164.9 30.2 %all-to-all-done = bf16[4,240,2048]{2,1,0:T(8,128)(2,1)} async-done(((bf16[4,240,2048]{2,1,0:T(8,128)(2,1)}), bf16[4,240,2048]{2,1,0:T(8,128)(2,1)}, u32[]{:S(2)}, u32[]{:S(2)}) %all-to-all-start) | async-done | bytes 3932192 | tf_op jit(solution)/shard_map/all_to_all | solution.py:118
  195.1 3.7 %gather_fusion.5 = bf16[75,2048]{1,0:T(8,128)(2,1)S(1)} fusion(bf16[960,2048]{1,0:T(8,128)(2,1)} %bitcast.6, s32[1024]{0:T(1024)S(1)} %pad_clamp_fusion), kind=kCustom, calls=%fused_computation.5 | custom fusion | bytes 614700 | tf_op jit(solution)/shard_map/gather | solution.py:125
  198.8 3.7 %gather_fusion.2 = bf16[75,2048]{1,0:T(8,128)(2,1)S(1)} fusion(bf16[960,2048]{1,0:T(8,128)(2,1)} %bitcast.6, s32[1024]{0:T(1024)S(1)} %pad_clamp_fusion.1), kind=kCustom, calls=%fused_computation.2 | custom fusion | bytes 614700 | tf_op jit(solution)/shard_map/gather | solution.py:125
  202.5 1.5 fusion.30
  204.0 1.5 fusion.25
  205.5 2.1 convolution_multiply_fusion
  207.7 2.1 convolution_multiply_fusion.1
  209.8 5.0 %scatter_custom_fusion = f32[960,2048]{1,0:T(8,128)} fusion(s32[75]{0:T(128)S(1)} %get-tuple-element.92, f32[75,2048]{1,0:T(8,128)S(1)} %convolution_multiply_fusion.1, f32[]{:T(128)} %constant.16.clone.1), kind=kCustom, calls=%fused_computation.23 | custom fusion | flops 153600 | bytes 7864324 | tf_op jit(solution)/shard_map/scatter-add | solution.py:131
  214.8 7.8 %scatter_fusion = f32[960,2048]{1,0:T(8,128)} fusion(f32[960,2048]{1,0:T(8,128)} %scatter_custom_fusion, s32[75]{0:T(128)S(1)} %get-tuple-element.90, f32[75,2048]{1,0:T(8,128)S(1)} %convolution_multiply_fusion), kind=kCustom, calls=%fused_computation.7 | custom fusion | flops 153600 | bytes 1843500 | tf_op jit(solution)/shard_map/scatter-add | solution.py:131
  222.6 0.0 reduce-scatter.5.cloned.1.call-update
  222.6 80.7 %reduce-scatter.5.cloned.1.call-done = f32[240,2048]{1,0:T(8,128)} async-done(((f32[960,2048]{1,0:T(8,128)}), f32[240,2048]{1,0:T(8,128)}) %reduce-scatter.5.cloned.1.call-update) | async-done | bytes 1966096 | tf_op jit(solution)/shard_map/reduce_scatter | solution.py:132
  303.3 2.7 fusion.16
  (27 shorter events, 0.2 us)
Async XLA Ops:
  6.5 6.7 %copy-start = (bf16[960,1024]{1,0:T(8,128)(2,1)S(1)}, bf16[960,1024]{1,0:T(8,128)(2,1)}, u32[]{:S(2)}) copy-start(bf16[960,1024]{1,0:T(8,128)(2,1)} %param.13) | copy-start | bytes 5898244
  6.5 132.2 %reduce-scatter.3.cloned.1.call-start = ((), (), s32[]{:S(2)}) async-start(), calls=%async_computation.3 | async-start | bytes 9830400 | tf_op jit(solution)/shard_map/reduce_scatter | solution.py:109
  17.2 0.7 copy-start.4
  17.2 1.0 copy-start.6
  53.4 85.4 %copy-start.1 = (bf16[240,2048]{1,0:T(8,128)(2,1)S(1)}, bf16[240,2048]{1,0:T(8,128)(2,1)}, u32[]{:S(2)}) copy-start(bf16[240,2048]{1,0:T(8,128)(2,1)} %param.16) | copy-start | bytes 2949124
  53.4 87.3 %copy-start.5 = (f32[2048]{0:T(1024)S(1)}, f32[2048]{0:T(1024)}, u32[]{:S(2)}) copy-start(f32[2048]{0:T(1024)} %param.18) | copy-start | bytes 24580
  143.4 5.7 %copy-start.2 = (s32[960,8]{0,1:T(8,128)S(1)}, s32[960,8]{0,1:T(8,128)}, u32[]{:S(2)}) copy-start(s32[960,8]{0,1:T(8,128)} %param.22) | copy-start | bytes 92164
  143.4 11.7 %copy-start.3 = (f32[960,8]{0,1:T(8,128)S(1)}, f32[960,8]{0,1:T(8,128)}, u32[]{:S(2)}) copy-start(f32[960,8]{0,1:T(8,128)} %param.23) | copy-start | bytes 92164
  143.4 51.7 %all-to-all-start = ((bf16[4,240,2048]{2,1,0:T(8,128)(2,1)}), bf16[4,240,2048]{2,1,0:T(8,128)(2,1)}, u32[]{:S(2)}, u32[]{:S(2)}) async-start(bf16[4,240,2048]{2,1,0:T(8,128)(2,1)} %stack.2), calls=%async_computation.1 | async-start | bytes 7864320 | tf_op jit(solution)/shard_map/all_to_all | solution.py:118
  149.1 154.2 %reduce-scatter.5.cloned.1.call-start = ((), (), s32[]{:S(2)}) async-start(), calls=%async_computation.4 | async-start | bytes 9830400 | tf_op jit(solution)/shard_map/reduce_scatter | solution.py:132
Sparse Core Ops, SparseCore 0:
  53.6 85.1 reduce-scatter.2
  222.7 80.5 reduce-scatter.4
